TPU v7x, 256 devices: a whole 4x4x8 slice. The times are simulated.
256 devices in a mesh: req: 128 (over y_hi, z, x, core), tp: 2 (over y_lo).
Axes of the slice: x: 4, y: 4 (y_hi: 2, y_lo: 2; y = y_hi * 2 + y_lo), z: 8, core: 2. Of those that a mesh axis runs over, the one named last changes fastest.
Arguments:
- tokens: bfloat16 [256, 512, 2048], P('req'), may hold values from -6 to 6
- qkv_master: float32 [2048, 3, 2048], P('req', None, 'tp')
- q_gain: float32 [2048], P('tp')
- k_gain: float32 [2048], P('tp')
- lengths: int32 [256], P('req'), may hold values from 1 to 512, as said below
- page_holder: int32 [256, 4], P('req'), may hold values from 0 to 127, as said below
- page_slot: int32 [256, 4], P('req'), may hold values from 0 to 2, as said below
Outputs:
- attended: bfloat16 [256, 512, 2048], P('req', None, 'tp')
- kv_cache: bfloat16 [1152, 2, 128, 2048], P('req', None, None, 'tp')
Inputs may be any that keep to these rules, and one draw needn't show every extreme that they name: lengths[r] is at least 1; some prompt has exactly 512 tokens. page_holder[r, p] is r // 2, or the index just before or just after it along req, cyclically. The live pages of one req index's prompts that go to one holder have distinct page_slot values, so at most 3 of them; some req index sends 3 live pages to one holder.
All inputs are finite; a program needn't handle non-finite values.
Results may differ from a plain program's by a relative error of at most 0.009.
Values may be sent and summed in bfloat16 or wider, within the bound.
No kernel may reach another device: no remote copies, remote signals or barrier semaphores. Data moves between devices by JAX's collectives and lax.ppermute only.
A program may use at most 128 MiB of HBM per device.

v0:
```python
import jax
import jax.numpy as jnp
from jax import lax
from jax.sharding import PartitionSpec as P

HD = 128
PAGE = 128
CAP = 3
SLOTS = 9
norm_epsilon = 1e-06
rope_theta = 500000.0


def extended(block, sides, width):
    for axis, dim in sides:
        count = lax.axis_size(axis)
        forward = [(i, i + 1) for i in range(count - 1)]
        forward.append((count - 1, 0))
        backward = [(target, source) for source, target in forward]
        low = lax.ppermute(
            lax.slice_in_dim(block, block.shape[dim] - width, None, axis=dim), axis, forward
        )
        high = lax.ppermute(lax.slice_in_dim(block, 0, width, axis=dim), axis, backward)
        block = jnp.concatenate([low, block, high], axis=dim)
    return block


def rotate(values_in, seq_len, head_size):
    half_size = head_size // 2
    positions = jnp.arange(seq_len).astype(jnp.float32)
    frequency = rope_theta ** (-jnp.arange(half_size).astype(jnp.float32) * 2.0 / head_size)
    angles = positions[:, None] * frequency[None, :]
    cosine_table = jnp.cos(angles)[:, None, :]
    sine_table = jnp.sin(angles)[:, None, :]
    front_half = values_in[..., :half_size]
    back_half = values_in[..., half_size:]
    return jnp.concatenate(
        [
            front_half * cosine_table - back_half * sine_table,
            back_half * cosine_table + front_half * sine_table,
        ],
        -1,
    )


def attend(request_item):
    queries, key_rows, value_rows, length = request_item
    seq_len = queries.shape[0]
    scores = jnp.einsum(
        "thd,uhd->htu", queries, key_rows, preferred_element_type=jnp.float32
    ) * HD ** (-0.5)
    query_pos = jnp.arange(seq_len)[:, None]
    key_pos = jnp.arange(seq_len)[None, :]
    allowed = (key_pos <= query_pos) & (key_pos < length)
    scores = jnp.where(allowed[None], scores, -1e30)
    row_max = jnp.max(scores, axis=-1, keepdims=True)
    exp_terms = jnp.where(allowed[None], jnp.exp(scores - row_max), 0.0)
    probs = (exp_terms / jnp.sum(exp_terms, axis=-1, keepdims=True)).astype(jnp.bfloat16)
    output = jnp.einsum("htu,uhd->thd", probs, value_rows, preferred_element_type=jnp.float32)
    keep_rows = jnp.arange(seq_len)[:, None, None] < length
    return jnp.where(keep_rows, output, 0.0).astype(jnp.bfloat16)


def body(tokens, qkv_master, q_gain, k_gain, lengths, page_holder, page_slot):
    req_dev, seq_len, model_width = tokens.shape
    row_share, _, q_local = qkv_master.shape
    heads_local = q_local // HD
    token_rows = tokens.reshape(req_dev * seq_len, model_width)
    master_local = qkv_master.astype(jnp.bfloat16).reshape(row_share, 3 * q_local)
    gathered = lax.all_gather(master_local, "req", axis=0, tiled=True)
    projected = jnp.dot(token_rows, gathered, preferred_element_type=jnp.float32)
    queries = projected[:, :q_local]
    key_rows = projected[:, q_local : 2 * q_local]
    values = projected[:, 2 * q_local :]
    square_sums = lax.psum((jnp.sum(queries * queries, -1), jnp.sum(key_rows * key_rows, -1)), "tp")
    full_width = q_local * lax.axis_size("tp")
    queries = queries * lax.rsqrt(square_sums[0] / full_width + norm_epsilon)[:, None] * q_gain
    key_rows = key_rows * lax.rsqrt(square_sums[1] / full_width + norm_epsilon)[:, None] * k_gain
    q_rot = rotate(queries.reshape(req_dev, seq_len, heads_local, HD), seq_len, HD).astype(
        jnp.bfloat16
    )
    k_rot = rotate(key_rows.reshape(req_dev, seq_len, heads_local, HD), seq_len, HD).astype(
        jnp.bfloat16
    )
    v_round = values.astype(jnp.bfloat16).reshape(req_dev, seq_len, heads_local, HD)
    attended = lax.map(attend, (q_rot, k_rot, v_round, lengths)).reshape(req_dev, seq_len, q_local)
    page_count = seq_len // PAGE
    home_index = lax.axis_index("req")
    axis_count = lax.axis_size("req")
    is_live = (jnp.arange(page_count) * PAGE)[None, :] < lengths[:, None]
    offset = (page_holder - home_index + 1 + axis_count) % axis_count - 1
    target = jnp.where(is_live, (offset + 1) * CAP + page_slot, -1).reshape(-1)
    onehot = (target[None, :] == jnp.arange(SLOTS)[:, None]).astype(jnp.bfloat16)
    stacked = jnp.stack(
        [
            k_rot.reshape(req_dev * page_count, PAGE * q_local),
            v_round.reshape(req_dev * page_count, PAGE * q_local),
        ],
        1,
    )
    stacked = stacked.reshape(req_dev * page_count, 2 * PAGE * q_local)
    outgoing = (
        jnp.dot(onehot, stacked, preferred_element_type=jnp.float32)
        .astype(jnp.bfloat16)
        .reshape(SLOTS, 2, PAGE, q_local)
    )
    padded = extended(outgoing, (("req", 0),), CAP)
    kv_cache = jnp.concatenate([padded[CAP + SLOTS :], outgoing[CAP : 2 * CAP], padded[:CAP]], 0)
    return (attended, kv_cache)


def solution(mesh):
    in_specs = (
        P("req", None, None),
        P("req", None, "tp"),
        P("tp"),
        P("tp"),
        P("req"),
        P("req", None),
        P("req", None),
    )
    out_specs = (P("req", None, "tp"), P("req", None, None, "tp"))
    return jax.shard_map(body, mesh=mesh, in_specs=in_specs, out_specs=out_specs, check_vma=False)
```

profile of v0, /device:TPU:8, one launch (start us, length us, event | category | flops | bytes accessed | tf_op | source)
XLA Modules:
  0.0 286.8 jit_solution(13818143167871856922)
XLA Ops:
  7.2 0.9 convert_bitcast_fusion
  8.2 0.6 copy.32
  8.9 0.8 compare_select_fusion.2
  9.7 1.0 multiply_cosine_fusion
  10.7 142.0 %all-gather.2.cloned.1.call-done = bf16[2048,3072]{1,0:T(8,128)(2,1)} async-done(((bf16[16,3072]{1,0:T(8,128)(2,1)}), bf16[2048,3072]{1,0:T(8,128)(2,1)}) %all-gather.2.cloned.1.call-update) | async-done | bytes 12582928 | tf_op jit(solution)/shard_map/all_gather | solution.py:70
  152.7 17.0 %fusion.26 = f32[1024,3072]{1,0:T(8,128)S(1)} fusion(bf16[1024,2048]{1,0:T(8,128)(2,1)} %bitcast.68, bf16[2048,3072]{1,0:T(8,128)(2,1)} %all-gather.2.cloned.1.call-done), kind=kOutput, calls=%fused_computation.61 | convolution fusion | flops 12884901888 | bytes 29360128 | tf_op jit(solution)/shard_map/dot_general | solution.py:71
  169.7 0.6 multiply_reduce_fusion
  170.8 3.4 %copy-done.1 = f32[1024,3072]{1,0:T(8,128)} copy-done((f32[1024,3072]{1,0:T(8,128)}, f32[1024,3072]{1,0:T(8,128)S(1)}, u32[]{:S(2)}) %copy-start.1) | copy-done | bytes 12582936
  174.6 1.9 copy.33
  176.5 5.0 %all-reduce = (f32[1024]{0:T(1024)S(1)}, f32[1024]{0:T(1024)S(1)}) all-reduce(f32[1024]{0:T(1024)S(1)} %get-tuple-element.48, f32[1024]{0:T(1024)S(1)} %get-tuple-element.47), channel_id=1, replica_groups=mesh['req'=128,'tp'=2] {'tp'}, use_global_device_ids=true, to_apply=%region_1.0 | all-reduce | flops 2048 | bytes 16384 | tf_op jit(solution)/shard_map/psum | solution.py:75
  181.5 5.3 %multiply_bitcast_fusion = (f32[128,8,8,128]{3,1,2,0:T(8,128)S(1)}, f32[128,8,8,128]{3,1,2,0:T(8,128)}) fusion(f32[1024,3072]{1,0:T(8,128)} %copy-done.1, f32[1024]{0:T(1024)S(1)} %copy-done.8, f32[1024]{0:T(1024)S(1)} %get-tuple-element.80, f32[1024]{0:T(1024)S(1)} %copy-done.9, f32[1024]{0:T(1024)S(1)} %get-tuple-element.81), kind=kLoop, calls=%fused_computation.32 | loop fusion | flops 4194304 | bytes 16793600
  186.8 3.0 %copy.35 = f32[128,8,8,128]{3,2,1,0:T(8,128)} copy(f32[128,8,8,128]{3,1,2,0:T(8,128)S(1)} %get-tuple-element.65) | data formatting | bytes 8388608
  189.7 2.3 stack_reshape_reshape.3
  192.0 3.2 %copy.34 = f32[128,8,8,128]{3,2,1,0:T(8,128)S(1)} copy(f32[128,8,8,128]{3,1,2,0:T(8,128)} %get-tuple-element.66) | data formatting | bytes 8388608
  195.2 4.7 %fusion.25 = (f32[2,512,8,64]{3,2,1,0:T(8,128)}, f32[2,512,8,64]{3,2,1,0:T(8,128)}) fusion(f32[2,512,8,128]{3,2,1,0:T(8,128)S(1)} %bitcast.59), kind=kLoop, calls=%fused_computation.59 | loop fusion | bytes 8388608 | tf_op jit(solution)/shard_map/slice | solution.py:35
  199.9 1.3 fusion.24
  201.3 1.7 multiply_subtract_fusion
  202.9 1.2 maximum_convert_fusion
  204.1 2.7 copy.24
  206.8 3.8 %convert_element_type.79 = bf16[8,1,131072]{2,0,1:T(8,128)(2,1)} reshape(bf16[2,512,8,128]{3,2,1,0:T(8,128)(2,1)} %copy.24) | data formatting | bytes 4194304 | tf_op jit(solution)/shard_map/convert_element_type | solution.py:82
  210.6 2.6 pad_maximum_fusion.1
  213.2 2.6 convolution_convert_fusion
  215.8 3.5 %fusion.23 = (bf16[3,262144]{1,0:T(4,128)(2,1)S(1)}, bf16[3,262144]{1,0:T(4,128)(2,1)S(1)}, bf16[3,262144]{1,0:T(4,128)(2,1)}) fusion(bf16[9,262144]{1,0:T(8,128)(2,1)S(1)} %convolution_convert_fusion), kind=kLoop, calls=%fused_computation.57 | loop fusion | bytes 9437184 | tf_op jit(solution)/shard_map/slice | solution.py:23
  219.3 1.8 copy.36
  221.0 1.8 copy.38
  222.8 7.5 %collective-permute-start = (bf16[3,2,128,1024]{3,2,1,0:T(8,128)(2,1)}, bf16[3,2,128,1024]{3,2,1,0:T(8,128)(2,1)}, u32[]{:S(2)}, u32[]{:S(2)}) collective-permute-start(bf16[3,2,128,1024]{3,2,1,0:T(8,128)(2,1)} %bitcast.24), channel_id=1, source_target_pairs={{2,0},{4,2},{6,4},{8,6},{10,8},{12,10},{14,12},{16,14},{18,16},{20... | collective-permute-start | bytes 4718600 | tf_op jit(solution)/shard_map/ppermute | solution.py:23
  230.3 1.7 subtract_convert_fusion
  232.0 2.5 pad_maximum_fusion.2
  234.4 37.0 %while.10 = (s32[]{:T(128)}, bf16[2,512,8,128]{1,3,2,0:T(8,128)(2,1)}, s32[2]{0:T(128)S(1)}, bf16[2,512,8,128]{3,2,1,0:T(8,128)(2,1)}, bf16[2,512,8,128]{3,1,2,0...) while((s32[]{:T(128)}, bf16[2,512,8,128]{1,3,2,0:T(8,128)(2,1)}, s32[2]{0:T(128)S(1)}, ...), condition=%wide.region_7.8_spmd, body=%wide.region_4.7_spmd.sunk | while | flops 1094190080 | bytes 63474368 | solution.py:86
  234.4 0.6 dynamic_slice.30
  235.0 0.6 iota_compare_fusion.5
  235.8 1.3 constant_dynamic-slice_fusion.2
  237.1 1.5 copy.48
  238.6 2.5 fusion.40
  241.1 6.3 %fusion.42 = (f32[8,512]{1,0:T(8,128)S(1)}, f32[8,512,512]{1,2,0:T(8,128)}) fusion(f32[8,512,512]{1,2,0:T(8,128)S(1)} %fusion.40, pred[512,512]{0,1:T(8,128)(4,1)S(1)} %fusion.41), kind=kOutput, calls=%fused_computation.56.clone.1 | output fusion | flops 14680575 | bytes 17055744 | tf_op jit(solution)/shard_map/while/body/eval_jaxpr/sub | solution.py:57
  247.4 4.2 %fusion.43 = bf16[2,512,8,128]{1,3,2,0:T(8,128)(2,1)S(1)} fusion(bf16[2,512,8,128]{1,3,2,0:T(8,128)(2,1)S(1)} %copy-done.6, s32[]{:T(128)S(6)} %copy.52, f32[8,512,512]{1,2,0:T(8,128)} %get-tuple-element.121, f32[8,512]{1,0:T(8,128)S(1)} %get-tuple-element.122, bf16[1,512,8,128]{1,3,2,0:T(8,128)(2,1)S(1)} %copy-done.2, ...), kind=kOutput, calls=%fused_computation.11.clone.1 | convolution fusion | flops 542113792 | bytes 10502660 | tf_op jit(solution)/shard_map/while/body/eval_jaxpr/htu,uhd->thd/dot_general | solution.py:59
  251.6 1.3 copy-done.7
  252.9 0.6 dynamic_slice.30
  253.5 0.6 iota_compare_fusion.5
  254.3 1.3 constant_dynamic-slice_fusion.2
  255.6 1.5 copy.48
  257.1 2.5 fusion.40
  259.6 6.3 %fusion.42 = (f32[8,512]{1,0:T(8,128)S(1)}, f32[8,512,512]{1,2,0:T(8,128)}) fusion(f32[8,512,512]{1,2,0:T(8,128)S(1)} %fusion.40, pred[512,512]{0,1:T(8,128)(4,1)S(1)} %fusion.41), kind=kOutput, calls=%fused_computation.56.clone.1 | output fusion | flops 14680575 | bytes 17055744 | tf_op jit(solution)/shard_map/while/body/eval_jaxpr/sub | solution.py:57
  265.9 4.2 %fusion.43 = bf16[2,512,8,128]{1,3,2,0:T(8,128)(2,1)S(1)} fusion(bf16[2,512,8,128]{1,3,2,0:T(8,128)(2,1)S(1)} %copy-done.6, s32[]{:T(128)S(6)} %copy.52, f32[8,512,512]{1,2,0:T(8,128)} %get-tuple-element.121, f32[8,512]{1,0:T(8,128)S(1)} %get-tuple-element.122, bf16[1,512,8,128]{1,3,2,0:T(8,128)(2,1)S(1)} %copy-done.2, ...), kind=kOutput, calls=%fused_computation.11.clone.1 | convolution fusion | flops 542113792 | bytes 10502660 | tf_op jit(solution)/shard_map/while/body/eval_jaxpr/htu,uhd->thd/dot_general | solution.py:59
  270.1 1.3 copy-done.7
  271.4 4.1 %copy.26 = bf16[2,512,1024]{2,1,0:T(8,128)(2,1)} copy(bf16[2,512,1024]{1,2,0:T(8,128)(2,1)} %bitcast.66) | data formatting | bytes 4194304 | tf_op jit(solution)/shard_map/reshape | solution.py:86
  275.5 0.6 copy.37
  276.1 3.8 %pad_maximum_fusion = bf16[9,2,128,1024]{3,2,1,0:T(8,128)(2,1)} fusion(bf16[3,2,128,1024]{3,2,1,0:T(8,128)(2,1)} %collective-permute-done.1, bf16[3,2,128,1024]{3,2,1,0:T(8,128)(2,1)S(1)} %bitcast.65, bf16[3,2,128,1024]{3,2,1,0:T(8,128)(2,1)} %collective-permute-done), kind=kLoop, calls=%fused_computation.26 | loop fusion | flops 4718592 | bytes 9437184 | tf_op jit(solution)/shard_map/concatenate | solution.py:108
  (40 shorter events, 1.3 us)
Async XLA Ops:
  7.2 145.5 %all-gather.2.cloned.1.call-start = ((), (), s32[]{:S(2)}) async-start(), calls=%async_computation | async-start | bytes 12681216 | tf_op jit(solution)/shard_map/all_gather | solution.py:70
  169.7 4.6 %copy-start.1 = (f32[1024,3072]{1,0:T(8,128)}, f32[1024,3072]{1,0:T(8,128)S(1)}, u32[]{:S(2)}) copy-start(f32[1024,3072]{1,0:T(8,128)S(1)} %fusion.26) | copy-start | bytes 37748740
  174.2 7.3 %copy-start.8 = (f32[1024]{0:T(1024)S(1)}, f32[1024]{0:T(1024)}, u32[]{:S(2)}) copy-start(f32[1024]{0:T(1024)} %param.12) | copy-start | bytes 12292
  174.2 7.3 %copy-start.9 = (f32[1024]{0:T(1024)S(1)}, f32[1024]{0:T(1024)}, u32[]{:S(2)}) copy-start(f32[1024]{0:T(1024)} %param.11) | copy-start | bytes 12292
  195.2 4.7 %copy-start = (f32[128,8,8,128]{3,2,1,0:T(8,128)S(1)}, f32[128,8,8,128]{3,2,1,0:T(8,128)}, u32[]{:S(2)}) copy-start(f32[128,8,8,128]{3,2,1,0:T(8,128)} %copy.35) | copy-start | bytes 12582916
  215.8 14.5 %copy-start.4 = (f32[2,512,8,64]{3,2,1,0:T(8,128)S(1)}, f32[2,512,8,64]{3,2,1,0:T(8,128)}, u32[]{:S(2)}) copy-start(f32[2,512,8,64]{3,2,1,0:T(8,128)} %get-tuple-element.77) | copy-start | bytes 6291460
  219.3 11.0 %copy-start.3 = (f32[2,512,8,64]{3,2,1,0:T(8,128)S(1)}, f32[2,512,8,64]{3,2,1,0:T(8,128)}, u32[]{:S(2)}) copy-start(f32[2,512,8,64]{3,2,1,0:T(8,128)} %get-tuple-element.76) | copy-start | bytes 6291460
  222.8 53.3 %collective-permute-start.1 = (bf16[3,2,128,1024]{3,2,1,0:T(8,128)(2,1)}, bf16[3,2,128,1024]{3,2,1,0:T(8,128)(2,1)}, u32[]{:S(2)}, u32[]{:S(2)}) collective-permute-start(bf16[3,2,128,1024]{3,2,1,0:T(8,128)(2,1)} %bitcast.30), channel_id=1, source_target_pairs={{0,2},{2,4},{4,6},{6,8},{8,10},{10,12},{12,14},{14,16},{16,18},{18... | collective-permute-start | bytes 4718600 | tf_op jit(solution)/shard_map/ppermute | solution.py:20
  222.8 53.3 %collective-permute-start = (bf16[3,2,128,1024]{3,2,1,0:T(8,128)(2,1)}, bf16[3,2,128,1024]{3,2,1,0:T(8,128)(2,1)}, u32[]{:S(2)}, u32[]{:S(2)}) collective-permute-start(bf16[3,2,128,1024]{3,2,1,0:T(8,128)(2,1)} %bitcast.24), channel_id=1, source_target_pairs={{2,0},{4,2},{6,4},{8,6},{10,8},{12,10},{14,12},{16,14},{18,16},{20... | collective-permute-start | bytes 4718600 | tf_op jit(solution)/shard_map/ppermute | solution.py:23
  231.9 2.5 copy-start.10
  241.1 6.3 %copy-start.2 = (bf16[1,512,8,128]{1,3,2,0:T(8,128)(2,1)S(1)}, bf16[1,512,8,128]{1,3,2,0:T(8,128)(2,1)}, u32[]{:S(2)}) copy-start(bf16[1,512,8,128]{1,3,2,0:T(8,128)(2,1)} %copy.48) | copy-start | bytes 3145732 | tf_op jit(solution)/shard_map/while
  241.1 6.3 %copy-start.6 = (bf16[2,512,8,128]{1,3,2,0:T(8,128)(2,1)S(1)}, bf16[2,512,8,128]{1,3,2,0:T(8,128)(2,1)}, u32[]{:S(2)}) copy-start(bf16[2,512,8,128]{1,3,2,0:T(8,128)(2,1)} %get-tuple-element.131) | copy-start | bytes 6291460 | tf_op jit(solution)/shard_map/while
  251.6 1.3 copy-start.7
  259.6 6.3 %copy-start.2 = (bf16[1,512,8,128]{1,3,2,0:T(8,128)(2,1)S(1)}, bf16[1,512,8,128]{1,3,2,0:T(8,128)(2,1)}, u32[]{:S(2)}) copy-start(bf16[1,512,8,128]{1,3,2,0:T(8,128)(2,1)} %copy.48) | copy-start | bytes 3145732 | tf_op jit(solution)/shard_map/while
  259.6 6.3 %copy-start.6 = (bf16[2,512,8,128]{1,3,2,0:T(8,128)(2,1)S(1)}, bf16[2,512,8,128]{1,3,2,0:T(8,128)(2,1)}, u32[]{:S(2)}) copy-start(bf16[2,512,8,128]{1,3,2,0:T(8,128)(2,1)} %get-tuple-element.131) | copy-start | bytes 6291460 | tf_op jit(solution)/shard_map/while
  270.1 1.3 copy-start.7
  271.4 4.1 %copy-start.5 = (bf16[3,262144]{1,0:T(4,128)(2,1)S(1)}, bf16[3,262144]{1,0:T(4,128)(2,1)}, u32[]{:S(2)}) copy-start(bf16[3,262144]{1,0:T(4,128)(2,1)} %get-tuple-element.73) | copy-start | bytes 4718596
Sparse Core Ops, SparseCore 0:
  12.4 140.2 all-gather.1
where the time goes:
time: 287 us
  waiting for transfers between devices  142 us (49%)
  local copies, waits for them, and re-layouts  49.1 us (17%)
  other arithmetic  36.1 us (13%)
  matrix products  32.9 us (11%)
  between operations  14.2 us (5%)
  starting transfers between devices  7.51 us (3%)
  blocking collectives  4.97 us (2%)
    all_gather x1, waiting for transfers between devices, body(): gathered = lax.all_gather(master_local, 'req', axis=0, tiled=True)  142 us
    dot_general x1, matrix products, body(): jnp.dot(token_rows, gathered, preferred_element_type=jnp.float32)  17 us
    unnamed x23, local copies, waits for them, and re-layouts  16.2 us
    sub x2, other arithmetic, attend(): exp_terms = jnp.where(allowed[None], jnp.exp(scores - row_max), 0.0)  12.6 us
    dot_general x2, matrix products, attend(): jnp.einsum('htu,uhd->thd', probs, value_rows, preferred_element_type=jnp....  8.38 us
    ppermute x1, starting transfers between devices, extended(): lax.ppermute(lax.slice_in_dim(block, 0, width, axis=dim), axis, backward)  7.47 us
    dynamic_slice x6, local copies, waits for them, and re-layouts, body(): lax.map(attend, (q_rot, k_rot, v_round, lengths))  6.79 us
    convert_element_type x2, local copies, waits for them, and re-layouts, body(): rotate(key_rows.reshape(req_dev, seq_len, heads_local, HD), seq_len, HD)  6.5 us
  transfers between devices with their start and end apart: 3, of which 1 were waited for; matrix products, arithmetic and copies ran while one was open for 16% of the time, Pallas kernels for 0%

commit v1 on v0

--- a/solution.py
+++ b/solution.py
@@ -9,6 +9,18 @@
 SLOTS = 9
 norm_epsilon = 1e-06
 rope_theta = 500000.0
+
+
+def sheets_get(ax_name, sample):
+    return jnp.concatenate(
+        lax.all_to_all(
+            jnp.stack(lax.axis_size(ax_name) * [sample]),
+            axis_name=ax_name,
+            split_axis=0,
+            concat_axis=0,
+        ),
+        axis=0,
+    )
 
 
 def extended(block, sides, width):
@@ -67,7 +79,7 @@
     heads_local = q_local // HD
     token_rows = tokens.reshape(req_dev * seq_len, model_width)
     master_local = qkv_master.astype(jnp.bfloat16).reshape(row_share, 3 * q_local)
-    gathered = lax.all_gather(master_local, "req", axis=0, tiled=True)
+    gathered = sheets_get("req", master_local)
     projected = jnp.dot(token_rows, gathered, preferred_element_type=jnp.float32)
     queries = projected[:, :q_local]
     key_rows = projected[:, q_local : 2 * q_local]

time: 287 us -> 436 us (1.52); the launches traced: 287 us -> 428 us
  waiting for transfers between devices: 142 us -> 276 us
  starting transfers between devices: 7.51 us -> 23 us
  between operations: 14.2 us -> 1.04 us
  local copies, waits for them, and re-layouts: 49.1 us -> 54.5 us
    all_to_all x0 -> x1, waiting for transfers between devices: none -> 276 us  [sheets_get(): lax.all_to_all(jnp.stack(lax.axis_size(ax_name) * [sample]), axis_name=ax...]
    all_gather x1 -> x0, waiting for transfers between devices: 142 us -> none  [body(): gathered = lax.all_gather(master_local, 'req', axis=0, tiled=True)]
    all_to_all x0 -> x1, starting transfers between devices: none -> 15.5 us  [sheets_get(): lax.all_to_all(jnp.stack(lax.axis_size(ax_name) * [sample]), axis_name=ax...]
    another operation x0 -> x2, local copies, waits for them, and re-layouts: none -> 6.08 us  [sheets_get(): jnp.stack(lax.axis_size(ax_name) * [sample])]
    unnamed x23 -> x27, local copies, waits for them, and re-layouts: 16.2 us -> 16.1 us
  transfers between devices with their start and end apart: 3 -> 3, of which waited for: 1 -> 1; matrix products, arithmetic and copies ran while one was open for 16% -> 10% of each run, Pallas kernels for 0% -> 0%
where the time goes in v1:
time: 436 us; the launch traced here: 428 us
  waiting for transfers between devices  276 us (63%)
  local copies, waits for them, and re-layouts  54.5 us (12%)
  other arithmetic  35.6 us (8%)
  matrix products  33.1 us (8%)
  starting transfers between devices  23 us (5%)
  blocking collectives  4.97 us (1%)
    all_to_all x1, waiting for transfers between devices, sheets_get(): lax.all_to_all(jnp.stack(lax.axis_size(ax_name) * [sample]), axis_name=ax...  276 us
    dot_general x1, matrix products, body(): jnp.dot(token_rows, gathered, preferred_element_type=jnp.float32)  17 us
    unnamed x27, local copies, waits for them, and re-layouts  16.1 us
    all_to_all x1, starting transfers between devices, sheets_get(): lax.all_to_all(jnp.stack(lax.axis_size(ax_name) * [sample]), axis_name=ax...  15.5 us
    sub x2, other arithmetic, attend(): exp_terms = jnp.where(allowed[None], jnp.exp(scores - row_max), 0.0)  12.5 us
  transfers between devices with their start and end apart: 3, of which 1 were waited for; matrix products, arithmetic and copies ran while one was open for 10% of the time, Pallas kernels for 0%

profile of v1, /device:TPU:8, one launch (start us, length us, event | category | flops | bytes accessed | tf_op | source)
XLA Modules:
  0.0 428.2 jit_solution(3179558541752282364)
XLA Ops:
  0.6 0.9 convert_bitcast_fusion
  1.6 6.1 %stack.6 = bf16[128,16,3072]{2,1,0:T(8,128)(2,1)} broadcast(bf16[16,3072]{1,0:T(8,128)(2,1)S(1)} %bitcast.68), dimensions={1,2} | broadcast | bytes 12681216 | tf_op jit(solution)/shard_map/stack | solution.py:17
  7.7 15.5 %all-to-all-start = ((bf16[128,16,3072]{2,1,0:T(8,128)(2,1)}), bf16[128,16,3072]{2,1,0:T(8,128)(2,1)}, u32[]{:S(2)}, u32[]{:S(2)}) async-start(bf16[128,16,3072]{2,1,0:T(8,128)(2,1)} %stack.6), calls=%async_computation | async-start | bytes 25165824 | tf_op jit(solution)/shard_map/all_to_all | solution.py:16
  23.4 1.0 multiply_cosine_fusion
  24.4 275.7 %all-to-all-done = bf16[128,16,3072]{2,1,0:T(8,128)(2,1)} async-done(((bf16[128,16,3072]{2,1,0:T(8,128)(2,1)}), bf16[128,16,3072]{2,1,0:T(8,128)(2,1)}, u32[]{:S(2)}, u32[]{:S(2)}) %all-to-all-start) | async-done | bytes 12582944 | tf_op jit(solution)/shard_map/all_to_all | solution.py:16
  300.1 17.0 %fusion.26 = f32[1024,3072]{1,0:T(8,128)S(1)} fusion(bf16[1024,2048]{1,0:T(8,128)(2,1)} %bitcast.69, bf16[2048,3072]{1,0:T(8,128)(2,1)} %bitcast.7), kind=kOutput, calls=%fused_computation.61 | convolution fusion | flops 12884901888 | bytes 29360128 | tf_op jit(solution)/shard_map/dot_general | solution.py:83
  317.1 0.6 multiply_reduce_fusion
  318.2 3.4 copy-done.1
  322.0 1.9 copy.33
  323.9 5.0 %all-reduce = (f32[1024]{0:T(1024)S(1)}, f32[1024]{0:T(1024)S(1)}) all-reduce(f32[1024]{0:T(1024)S(1)} %get-tuple-element.48, f32[1024]{0:T(1024)S(1)} %get-tuple-element.47), channel_id=1, replica_groups=mesh['req'=128,'tp'=2] {'tp'}, use_global_device_ids=true, to_apply=%region_1.0 | all-reduce | flops 2048 | bytes 16384 | tf_op jit(solution)/shard_map/psum | solution.py:87
  328.9 5.5 %multiply_bitcast_fusion = (f32[128,8,8,128]{3,1,2,0:T(8,128)S(1)}, f32[128,8,8,128]{3,1,2,0:T(8,128)}) fusion(f32[1024,3072]{1,0:T(8,128)} %copy-done.1, f32[1024]{0:T(1024)S(1)} %copy-done.8, f32[1024]{0:T(1024)S(1)} %get-tuple-element.80, f32[1024]{0:T(1024)S(1)} %copy-done.9, f32[1024]{0:T(1024)S(1)} %get-tuple-element.81), kind=kLoop, calls=%fused_computation.32 | loop fusion | flops 4194304 | bytes 16793600
  334.4 3.0 copy.35
  337.4 2.3 stack_reshape_reshape.3
  339.7 3.2 copy.34
  342.9 4.7 %fusion.25 = (f32[2,512,8,64]{3,2,1,0:T(8,128)}, f32[2,512,8,64]{3,2,1,0:T(8,128)}) fusion(f32[2,512,8,128]{3,2,1,0:T(8,128)S(1)} %bitcast.60), kind=kLoop, calls=%fused_computation.59 | loop fusion | bytes 8388608 | tf_op jit(solution)/shard_map/slice | solution.py:47
  347.6 1.3 fusion.24
  349.0 1.7 multiply_subtract_fusion
  350.6 1.2 maximum_convert_fusion
  351.8 2.7 copy.24
  354.5 3.8 convert_element_type.79
  358.3 2.6 pad_maximum_fusion.1
  360.9 2.8 convolution_convert_fusion
  363.7 3.4 fusion.23
  367.2 1.7 copy.36
  368.9 1.7 copy.38
  370.7 7.5 %collective-permute-start = (bf16[3,2,128,1024]{3,2,1,0:T(8,128)(2,1)}, bf16[3,2,128,1024]{3,2,1,0:T(8,128)(2,1)}, u32[]{:S(2)}, u32[]{:S(2)}) collective-permute-start(bf16[3,2,128,1024]{3,2,1,0:T(8,128)(2,1)} %bitcast.25), channel_id=1, source_target_pairs={{2,0},{4,2},{6,4},{8,6},{10,8},{12,10},{14,12},{16,14},{18,16},{20... | collective-permute-start | bytes 4718600 | tf_op jit(solution)/shard_map/ppermute | solution.py:35
  378.1 1.7 subtract_convert_fusion
  379.8 2.5 pad_maximum_fusion.2
  382.3 37.2 %while.10 = (s32[]{:T(128)}, bf16[2,512,8,128]{1,3,2,0:T(8,128)(2,1)}, s32[2]{0:T(128)S(1)}, bf16[2,512,8,128]{3,2,1,0:T(8,128)(2,1)}, bf16[2,512,8,128]{3,1,2,0...) while((s32[]{:T(128)}, bf16[2,512,8,128]{1,3,2,0:T(8,128)(2,1)}, s32[2]{0:T(128)S(1)}, ...), condition=%wide.region_7.8_spmd, body=%wide.region_4.7_spmd.sunk | while | flops 1094190080 | bytes 63474368 | solution.py:98
  382.4 0.6 dynamic_slice.30
  383.0 0.6 iota_compare_fusion.5
  383.8 1.3 constant_dynamic-slice_fusion.2
  385.1 1.5 copy.48
  386.6 2.5 fusion.40
  389.1 6.3 %fusion.42 = (f32[8,512]{1,0:T(8,128)S(1)}, f32[8,512,512]{1,2,0:T(8,128)}) fusion(f32[8,512,512]{1,2,0:T(8,128)S(1)} %fusion.40, pred[512,512]{0,1:T(8,128)(4,1)S(1)} %fusion.41), kind=kOutput, calls=%fused_computation.56.clone.1 | output fusion | flops 14680575 | bytes 17055744 | tf_op jit(solution)/shard_map/while/body/eval_jaxpr/sub | solution.py:69
  395.4 4.2 fusion.43
  399.6 1.4 copy-done.7
  400.9 0.6 dynamic_slice.30
  401.6 0.6 iota_compare_fusion.5
  402.3 1.3 constant_dynamic-slice_fusion.2
  403.6 1.5 copy.48
  405.1 2.5 fusion.40
  407.6 6.3 %fusion.42 = (f32[8,512]{1,0:T(8,128)S(1)}, f32[8,512,512]{1,2,0:T(8,128)}) fusion(f32[8,512,512]{1,2,0:T(8,128)S(1)} %fusion.40, pred[512,512]{0,1:T(8,128)(4,1)S(1)} %fusion.41), kind=kOutput, calls=%fused_computation.56.clone.1 | output fusion | flops 14680575 | bytes 17055744 | tf_op jit(solution)/shard_map/while/body/eval_jaxpr/sub | solution.py:69
  413.9 4.2 fusion.43
  418.1 1.4 copy-done.7
  419.5 4.1 copy.26
  423.5 0.6 copy.37
  424.2 3.8 pad_maximum_fusion
  (44 shorter events, 1.4 us)
Async XLA Ops:
  7.7 15.5 %copy-start.10 = (s32[2,4]{1,0:T(2,128)S(1)}, s32[2,4]{1,0:T(2,128)}, u32[]{:S(2)}) copy-start(s32[2,4]{1,0:T(2,128)} %param.15) | copy-start | bytes 100
  7.7 15.5 %copy-start.11 = (s32[2,4]{1,0:T(2,128)S(1)}, s32[2,4]{1,0:T(2,128)}, u32[]{:S(2)}) copy-start(s32[2,4]{1,0:T(2,128)} %param.14) | copy-start | bytes 100
  7.7 15.5 %copy-start.12 = (s32[2]{0:T(128)S(1)}, s32[2]{0:T(128)}, u32[]{:S(2)}) copy-start(s32[2]{0:T(128)} %param.13) | copy-start | bytes 28
  7.7 292.4 %all-to-all-start = ((bf16[128,16,3072]{2,1,0:T(8,128)(2,1)}), bf16[128,16,3072]{2,1,0:T(8,128)(2,1)}, u32[]{:S(2)}, u32[]{:S(2)}) async-start(bf16[128,16,3072]{2,1,0:T(8,128)(2,1)} %stack.6), calls=%async_computation | async-start | bytes 25165824 | tf_op jit(solution)/shard_map/all_to_all | solution.py:16
  317.1 4.5 %copy-start.1 = (f32[1024,3072]{1,0:T(8,128)}, f32[1024,3072]{1,0:T(8,128)S(1)}, u32[]{:S(2)}) copy-start(f32[1024,3072]{1,0:T(8,128)S(1)} %fusion.26) | copy-start | bytes 37748740
  321.6 7.3 %copy-start.8 = (f32[1024]{0:T(1024)S(1)}, f32[1024]{0:T(1024)}, u32[]{:S(2)}) copy-start(f32[1024]{0:T(1024)} %param.12) | copy-start | bytes 12292
  321.6 7.3 %copy-start.9 = (f32[1024]{0:T(1024)S(1)}, f32[1024]{0:T(1024)}, u32[]{:S(2)}) copy-start(f32[1024]{0:T(1024)} %param.11) | copy-start | bytes 12292
  342.9 4.7 %copy-start = (f32[128,8,8,128]{3,2,1,0:T(8,128)S(1)}, f32[128,8,8,128]{3,2,1,0:T(8,128)}, u32[]{:S(2)}) copy-start(f32[128,8,8,128]{3,2,1,0:T(8,128)} %copy.35) | copy-start | bytes 12582916
  363.7 14.4 %copy-start.4 = (f32[2,512,8,64]{3,2,1,0:T(8,128)S(1)}, f32[2,512,8,64]{3,2,1,0:T(8,128)}, u32[]{:S(2)}) copy-start(f32[2,512,8,64]{3,2,1,0:T(8,128)} %get-tuple-element.77) | copy-start | bytes 6291460
  367.2 11.0 %copy-start.3 = (f32[2,512,8,64]{3,2,1,0:T(8,128)S(1)}, f32[2,512,8,64]{3,2,1,0:T(8,128)}, u32[]{:S(2)}) copy-start(f32[2,512,8,64]{3,2,1,0:T(8,128)} %get-tuple-element.76) | copy-start | bytes 6291460
  370.6 53.5 %collective-permute-start.1 = (bf16[3,2,128,1024]{3,2,1,0:T(8,128)(2,1)}, bf16[3,2,128,1024]{3,2,1,0:T(8,128)(2,1)}, u32[]{:S(2)}, u32[]{:S(2)}) collective-permute-start(bf16[3,2,128,1024]{3,2,1,0:T(8,128)(2,1)} %bitcast.31), channel_id=1, source_target_pairs={{0,2},{2,4},{4,6},{6,8},{8,10},{10,12},{12,14},{14,16},{16,18},{18... | collective-permute-start | bytes 4718600 | tf_op jit(solution)/shard_map/ppermute | solution.py:32
  370.7 53.5 %collective-permute-start = (bf16[3,2,128,1024]{3,2,1,0:T(8,128)(2,1)}, bf16[3,2,128,1024]{3,2,1,0:T(8,128)(2,1)}, u32[]{:S(2)}, u32[]{:S(2)}) collective-permute-start(bf16[3,2,128,1024]{3,2,1,0:T(8,128)(2,1)} %bitcast.25), channel_id=1, source_target_pairs={{2,0},{4,2},{6,4},{8,6},{10,8},{12,10},{14,12},{16,14},{18,16},{20... | collective-permute-start | bytes 4718600 | tf_op jit(solution)/shard_map/ppermute | solution.py:35
  389.1 6.3 %copy-start.2 = (bf16[1,512,8,128]{1,3,2,0:T(8,128)(2,1)S(1)}, bf16[1,512,8,128]{1,3,2,0:T(8,128)(2,1)}, u32[]{:S(2)}) copy-start(bf16[1,512,8,128]{1,3,2,0:T(8,128)(2,1)} %copy.48) | copy-start | bytes 3145732 | tf_op jit(solution)/shard_map/while
  389.1 6.3 %copy-start.6 = (bf16[2,512,8,128]{1,3,2,0:T(8,128)(2,1)S(1)}, bf16[2,512,8,128]{1,3,2,0:T(8,128)(2,1)}, u32[]{:S(2)}) copy-start(bf16[2,512,8,128]{1,3,2,0:T(8,128)(2,1)} %get-tuple-element.131) | copy-start | bytes 6291460 | tf_op jit(solution)/shard_map/while
  399.6 1.4 copy-start.7
  407.6 6.3 %copy-start.2 = (bf16[1,512,8,128]{1,3,2,0:T(8,128)(2,1)S(1)}, bf16[1,512,8,128]{1,3,2,0:T(8,128)(2,1)}, u32[]{:S(2)}) copy-start(bf16[1,512,8,128]{1,3,2,0:T(8,128)(2,1)} %copy.48) | copy-start | bytes 3145732 | tf_op jit(solution)/shard_map/while
  407.6 6.3 %copy-start.6 = (bf16[2,512,8,128]{1,3,2,0:T(8,128)(2,1)S(1)}, bf16[2,512,8,128]{1,3,2,0:T(8,128)(2,1)}, u32[]{:S(2)}) copy-start(bf16[2,512,8,128]{1,3,2,0:T(8,128)(2,1)} %get-tuple-element.131) | copy-start | bytes 6291460 | tf_op jit(solution)/shard_map/while
  418.1 1.4 copy-start.7
  419.5 4.1 copy-start.5
